TPU v7x, 256 devices: a whole 4x4x8 slice. The times are simulated.
256 devices in a mesh: row: 16 (over z_lo, y), col: 8 (over x, core), layer: 2 (over z_hi).
Axes of the slice: x: 4, y: 4, z: 8 (z_hi: 2, z_lo: 4; z = z_hi * 4 + z_lo), core: 2. Of those that a mesh axis runs over, the one named last changes fastest.
Arguments:
- density: float32 [2, 8192, 2048], P('layer', 'row', 'col'), may hold values from -6 to 6
- dens_mask: int32 [2, 128, 32], P('layer', 'row', 'col'), may hold values from 0 to 1, as said below
- hamiltonian: float32 [2, 2048, 16384], P('layer', 'row', 'col'), may hold values from -0.375 to 0.375
- ham_mask: int32 [2, 32, 256], P('layer', None, 'col'), may hold values from 0 to 1, as said below
- filter_mask: int32 [128, 256], P('row', 'col'), may hold values from 0 to 1, as said below
Outputs:
- product: float32 [8192, 16384], P('row', ('col', 'layer'))
Inputs may be any that keep to these rules, and one draw needn't show every extreme that they name: `dens_mask`: 1 where a density block is nonzero, else 0. `ham_mask`: 1 where a Hamiltonian block is nonzero, else 0. `filter_mask`: 1 where a result block is kept, else 0.
All inputs are finite; a program needn't handle non-finite values.
Results may differ from a plain program's by a relative error of at most 0.0001.
Values sent between devices are 32-bit elements; how exact they have to be, the bound alone decides.
No kernel may reach another device: no remote copies, remote signals or barrier semaphores. Data moves between devices by JAX's collectives and lax.ppermute only.
A program may use at most 128 MiB of HBM per device.

v0:
```python
import jax
import jax.numpy as jnp
from jax import lax
from jax.sharding import Mesh
from jax.sharding import PartitionSpec as P

BLOCK = 64
AXES = ("zl", "yh", "yl", "x", "core", "layer")
ROW = ("zl", "yh", "yl")
COL = ("x", "core")


def expand(block_mask):
    widened = jnp.repeat(block_mask.astype(jnp.float32), BLOCK, axis=-2)
    return jnp.repeat(widened, BLOCK, axis=-1)


def product_dot(a, b):
    return jnp.dot(a, b, precision=lax.Precision.HIGH, preferred_element_type=jnp.float32)


def gather_cols(block, index, n):
    parts = [block]
    for shift in range(1, n):
        parts.append(lax.ppermute(block, COL, [((i + shift) % n, i) for i in range(n)]))
    twice = jnp.concatenate(parts + parts, axis=1)
    return lax.dynamic_slice_in_dim(twice, (n - index) * block.shape[1], n * block.shape[1], axis=1)


def shards(density, dens_mask, hamiltonian, ham_mask, filter_mask, n_col):
    yl = lax.axis_index("yl")
    core = lax.axis_index("core")
    layer = lax.axis_index("layer")
    row = (lax.axis_index("zl") * 2 + lax.axis_index("yh")) * 2 + yl
    col = lax.axis_index("x") * 2 + core
    dens_vals = (density * expand(dens_mask))[0]
    ham_count = hamiltonian.shape[1]
    picked = lax.dynamic_slice_in_dim(
        ham_mask[0], row * (ham_count // BLOCK), ham_count // BLOCK, axis=0
    )
    ham_vals = hamiltonian[0] * expand(picked)
    half = ham_vals.shape[1] // 2
    kept = lax.dynamic_slice_in_dim(expand(filter_mask), layer * half, half, axis=1)
    pieces = {}
    for h in (0, 1):
        part = ham_vals[:, h * half : (h + 1) * half]
        for j in (0, 1):
            pieces[h, j] = lax.ppermute(
                part, ("yl", "core"), [(j * 2 + c, c * 2 + h) for c in (0, 1)]
            )
    contrib = jnp.where(
        core == 0,
        jnp.concatenate([pieces[0, 0], pieces[0, 1]], axis=0),
        jnp.concatenate([pieces[1, 0], pieces[1, 1]], axis=0),
    )
    ham_own = lax.all_gather(contrib, ("zl", "yh"), axis=0, tiled=True)
    ham_other = lax.ppermute(ham_own, "core", [(0, 1), (1, 0)])
    dens_own = gather_cols(dens_vals, col, n_col)
    dens_nbr = lax.ppermute(dens_own, ("yl", "core"), [(0, 2), (3, 1)])
    dens_rows = jnp.where(core == yl, dens_own, dens_nbr)
    part_own = product_dot(dens_rows, ham_own)
    part_other = product_dot(dens_rows, ham_other)

    def route(value, target_layer):
        perm = []
        for j in (0, 1):
            for k in (0, 1):
                for src in (0, 1):
                    perm.append((j * 4 + k * 2 + src, k * 4 + j * 2 + target_layer(k)))
        return [
            lax.ppermute(value, ("yl", "core", "layer"), [p for p in perm if p[0] % 2 == src])
            for src in (0, 1)
        ]

    got = route(part_own, lambda k: k) + route(part_other, lambda k: 1 - k)
    total = got[0] + got[1] + (got[2] + got[3])
    return total * kept


def solution(mesh):
    rows, cols, layers = mesh.devices.shape
    fine = Mesh(mesh.devices.reshape(rows // 4, 2, 2, cols // 2, 2, layers), AXES)
    return jax.shard_map(
        lambda *args: shards(*args, cols),
        mesh=fine,
        in_specs=(
            P("layer", ROW, COL),
            P("layer", ROW, COL),
            P("layer", ROW, COL),
            P("layer", None, COL),
            P(ROW, COL),
        ),
        out_specs=P(ROW, ("x", "core", "layer")),
        check_vma=False,
    )
```

profile of v0, /device:TPU:104, one launch (start us, length us, event | category | flops | bytes accessed | tf_op | source)
XLA Modules:
  0.0 483.6 jit_solution(13155475771516272750)
XLA Ops:
  6.5 0.8 convert_bitcast_fusion.1
  7.6 1.6 copy.8
  9.3 0.7 collective-permute-start.10
  10.0 4.3 collective-permute-start.11
  14.3 1.3 collective-permute-start.8
  15.6 1.9 collective-permute-start.9
  17.6 3.4 collective-permute-done.11
  21.0 3.9 collective-permute-done.8
  24.8 1.8 collective-permute-done.9
  26.6 2.1 maximum_select_fusion
  28.7 177.7 %all-gather.2.cloned.1.call-done = f32[2048,1024]{0,1:T(8,128)} async-done(((f32[256,1024]{0,1:T(8,128)}), f32[2048,1024]{0,1:T(8,128)}) %all-gather.2.cloned.1.call-update) | async-done | bytes 8388624 | tf_op jit(solution)/shard_map/all_gather | solution.py:56
  206.8 1.0 constant_dynamic-update-slice_fusion.15
  207.8 2.8 collective-permute-start
  210.6 0.9 collective-permute-start.1
  211.5 2.4 collective-permute-start.3
  213.9 9.1 %collective-permute-done = f32[512,256]{0,1:T(8,128)S(1)} collective-permute-done((f32[512,256]{0,1:T(8,128)S(1)}, f32[512,256]{0,1:T(8,128)S(1)}, u32[]{:S(2)}, u32[]{:S(2)}) %collective-permute-start) | collective-permute-done | bytes 524320 | tf_op jit(solution)/shard_map/ppermute | solution.py:25
  222.9 1.0 collective-permute-start.4
  223.9 32.2 %collective-permute-done.1 = f32[512,256]{0,1:T(8,128)S(1)} collective-permute-done((f32[512,256]{0,1:T(8,128)S(1)}, f32[512,256]{0,1:T(8,128)S(1)}, u32[]{:S(2)}, u32[]{:S(2)}) %collective-permute-start.1) | collective-permute-done | bytes 524320 | tf_op jit(solution)/shard_map/ppermute | solution.py:25
  256.1 0.8 constant_dynamic-update-slice_fusion.14
  256.9 0.8 constant_dynamic-update-slice_fusion.13
  257.8 0.8 constant_dynamic-update-slice_fusion.12
  258.6 0.8 constant_dynamic-update-slice_fusion.11
  259.4 0.8 constant_dynamic-update-slice_fusion.10
  260.3 12.1 %collective-permute-done.5 = f32[512,256]{0,1:T(8,128)S(1)} collective-permute-done((f32[512,256]{0,1:T(8,128)S(1)}, f32[512,256]{0,1:T(8,128)S(1)}, u32[]{:S(2)}, u32[]{:S(2)}) %collective-permute-start.5) | collective-permute-done | bytes 524320 | tf_op jit(solution)/shard_map/ppermute | solution.py:25
  272.4 0.8 constant_dynamic-update-slice_fusion.9
  273.2 0.8 constant_dynamic-update-slice_fusion.8
  274.0 0.8 constant_dynamic-update-slice_fusion.7
  274.9 0.8 constant_dynamic-update-slice_fusion.6
  275.7 0.8 constant_dynamic-update-slice_fusion.5
  276.6 0.9 constant_dynamic-update-slice_fusion.4
  277.4 0.8 constant_dynamic-update-slice_fusion.3
  278.3 0.8 constant_dynamic-update-slice_fusion.2
  279.1 0.8 constant_dynamic-update-slice_fusion.1
  279.9 0.9 constant_dynamic-update-slice_fusion
  280.8 4.6 constant_dynamic-slice_fusion.1
  285.4 1.5 collective-permute-start.7
  286.9 49.2 %collective-permute-done.7 = f32[512,2048]{0,1:T(8,128)} collective-permute-done((f32[512,2048]{0,1:T(8,128)}, f32[512,2048]{0,1:T(8,128)}, u32[]{:S(2)}, u32[]{:S(2)}) %collective-permute-start.7) | collective-permute-done | bytes 4194336 | tf_op jit(solution)/shard_map/ppermute | solution.py:59
  336.1 17.9 %fusion.1 = f32[512,1024]{1,0:T(8,128)} fusion(f32[2048,1024]{0,1:T(8,128)} %all-gather.2.cloned.1.call-done, f32[512,2048]{0,1:T(8,128)} %constant_dynamic-slice_fusion.1, f32[512,2048]{0,1:T(8,128)} %collective-permute-done.7, pred[]{:T(512)S(6)} %eq.6), kind=kOutput, calls=%fused_computation.3 | convolution fusion | flops 6443499520 | bytes 18874368 | tf_op jit(solution)/shard_map/dot_general | solution.py:19
  354.0 2.8 collective-permute-start.12
  356.8 2.0 collective-permute-start.13
  358.8 17.9 %fusion = f32[512,1024]{1,0:T(8,128)} fusion(f32[2048,1024]{0,1:T(8,128)} %collective-permute-done.14, f32[512,2048]{0,1:T(8,128)} %constant_dynamic-slice_fusion.1, f32[512,2048]{0,1:T(8,128)} %collective-permute-done.7, pred[]{:T(512)S(6)} %eq.6), kind=kOutput, calls=%fused_computation.2 | convolution fusion | flops 6443499520 | bytes 18874368 | tf_op jit(solution)/shard_map/dot_general | solution.py:19
  376.7 3.6 collective-permute-start.15
  380.4 1.3 collective-permute-start.16
  382.7 1.8 copy.12
  384.5 4.3 collective-permute-done.12
  388.7 54.1 %collective-permute-done.15 = f32[512,1024]{1,0:T(8,128)} collective-permute-done((f32[512,1024]{1,0:T(8,128)}, f32[512,1024]{1,0:T(8,128)}, u32[]{:S(2)}, u32[]{:S(2)}) %collective-permute-start.15) | collective-permute-done | bytes 2097184 | tf_op jit(solution)/shard_map/ppermute | solution.py:71
  442.8 27.2 %collective-permute-done.16 = f32[512,1024]{1,0:T(8,128)} collective-permute-done((f32[512,1024]{1,0:T(8,128)}, f32[512,1024]{1,0:T(8,128)}, u32[]{:S(2)}, u32[]{:S(2)}) %collective-permute-start.16) | collective-permute-done | bytes 2097184 | tf_op jit(solution)/shard_map/ppermute | solution.py:71
  470.0 6.8 %add_multiply_fusion = f32[512,1024]{1,0:T(8,128)} fusion(f32[512,1024]{1,0:T(8,128)} %copy.12, f32[512,1024]{1,0:T(8,128)} %collective-permute-done.15, f32[512,1024]{1,0:T(8,128)} %collective-permute-done.16, f32[512,1024]{1,0:T(8,128)} %collective-permute-done.12, f32[512,1024]{1,0:T(8,128)} %collective-permute-done.13), kind=kLoop, calls=%fused_computation | loop fusion | flops 2097152 | bytes 12582912 | tf_op jit(solution)/shard_map/mul | solution.py:77
  (34 shorter events, 1.8 us)
Async XLA Ops:
  6.5 199.9 %copy-start = (f32[1,512,256]{2,1,0:T(8,128)S(1)}, f32[1,512,256]{2,1,0:T(8,128)}, u32[]{:S(2)}) copy-start(f32[1,512,256]{2,1,0:T(8,128)} %param.5) | copy-start | bytes 1572868
  6.5 200.1 %copy-start.2 = (s32[1,8,4]{1,2,0:T(4,128)S(1)}, s32[1,8,4]{1,2,0:T(4,128)}, u32[]{:S(2)}) copy-start(s32[1,8,4]{1,2,0:T(4,128)} %param.6) | copy-start | bytes 388
  6.5 199.9 %all-gather.2.cloned.1.call-start = ((), (), s32[]{:S(2)}) async-start(), calls=%async_computation | async-start | bytes 9437184 | tf_op jit(solution)/shard_map/all_gather | solution.py:56
  9.3 8.3 %collective-permute-start.10 = (f32[128,1024]{0,1:T(8,128)S(1)}, f32[128,1024]{0,1:T(8,128)S(1)}, u32[]{:S(2)}, u32[]{:S(2)}) collective-permute-start(f32[128,1024]{0,1:T(8,128)S(1)} %get-tuple-element.5), channel_id=1, source_target_pairs={{0,2},{2,18},{1,3},{3,19},{4,6},{6,22},{5,7},{7,23},{8,10},{10,26}... | collective-permute-start | bytes 1572872 | tf_op jit(solution)/shard_map/ppermute | solution.py:48
  10.0 11.0 %collective-permute-start.11 = (f32[128,1024]{0,1:T(8,128)S(1)}, f32[128,1024]{0,1:T(8,128)S(1)}, u32[]{:S(2)}, u32[]{:S(2)}) collective-permute-start(f32[128,1024]{0,1:T(8,128)S(1)} %get-tuple-element.5), channel_id=1, source_target_pairs={{16,2},{18,18},{17,3},{19,19},{20,6},{22,22},{21,7},{23,23},{24,10... | collective-permute-start | bytes 1572872 | tf_op jit(solution)/shard_map/ppermute | solution.py:48
  14.3 10.5 %collective-permute-start.8 = (f32[128,1024]{0,1:T(8,128)S(1)}, f32[128,1024]{0,1:T(8,128)S(1)}, u32[]{:S(2)}, u32[]{:S(2)}) collective-permute-start(f32[128,1024]{0,1:T(8,128)S(1)} %get-tuple-element.6), channel_id=1, source_target_pairs={{0,0},{2,16},{1,1},{3,17},{4,4},{6,20},{5,5},{7,21},{8,8},{10,24},... | collective-permute-start | bytes 1572872 | tf_op jit(solution)/shard_map/ppermute | solution.py:48
  15.6 11.0 %collective-permute-start.9 = (f32[128,1024]{0,1:T(8,128)S(1)}, f32[128,1024]{0,1:T(8,128)}, u32[]{:S(2)}, u32[]{:S(2)}) collective-permute-start(f32[128,1024]{0,1:T(8,128)S(1)} %get-tuple-element.6), channel_id=1, source_target_pairs={{16,0},{18,16},{17,1},{19,17},{20,4},{22,20},{21,5},{23,21},{24,8}... | collective-permute-start | bytes 1572872 | tf_op jit(solution)/shard_map/ppermute | solution.py:48
  206.5 152.4 %collective-permute-start.14 = (f32[2048,1024]{0,1:T(8,128)}, f32[2048,1024]{0,1:T(8,128)}, u32[]{:S(2)}, u32[]{:S(2)}) collective-permute-start(f32[2048,1024]{0,1:T(8,128)} %all-gather.2.cloned.1.call-done), channel_id=1, source_target_pairs={{0,2},{2,0},{1,3},{3,1},{4,6},{6,4},{5,7},{7,5},{8,10},{10,8},{9,1... | collective-permute-start | bytes 25165832 | tf_op jit(solution)/shard_map/ppermute | solution.py:57
  207.8 15.1 %collective-permute-start = (f32[512,256]{0,1:T(8,128)S(1)}, f32[512,256]{0,1:T(8,128)S(1)}, u32[]{:S(2)}, u32[]{:S(2)}) collective-permute-start(f32[512,256]{0,1:T(8,128)S(1)} %bitcast.23), channel_id=1, source_target_pairs={{2,0},{4,2},{6,4},{8,6},{10,8},{12,10},{14,12},{0,14},{3,1},{5,3},... | collective-permute-start | bytes 1572872 | tf_op jit(solution)/shard_map/ppermute | solution.py:25
  210.6 45.5 %collective-permute-start.1 = (f32[512,256]{0,1:T(8,128)S(1)}, f32[512,256]{0,1:T(8,128)S(1)}, u32[]{:S(2)}, u32[]{:S(2)}) collective-permute-start(f32[512,256]{0,1:T(8,128)S(1)} %bitcast.24), channel_id=1, source_target_pairs={{4,0},{6,2},{8,4},{10,6},{12,8},{14,10},{0,12},{2,14},{5,1},{7,3},... | collective-permute-start | bytes 1572872 | tf_op jit(solution)/shard_map/ppermute | solution.py:25
  211.5 45.5 %collective-permute-start.2 = (f32[512,256]{0,1:T(8,128)S(1)}, f32[512,256]{0,1:T(8,128)S(1)}, u32[]{:S(2)}, u32[]{:S(2)}) collective-permute-start(f32[512,256]{0,1:T(8,128)S(1)} %bitcast.25), channel_id=1, source_target_pairs={{6,0},{8,2},{10,4},{12,6},{14,8},{0,10},{2,12},{4,14},{7,1},{9,3},... | collective-permute-start | bytes 1572872 | tf_op jit(solution)/shard_map/ppermute | solution.py:25
  211.5 47.1 %collective-permute-start.3 = (f32[512,256]{0,1:T(8,128)S(1)}, f32[512,256]{0,1:T(8,128)S(1)}, u32[]{:S(2)}, u32[]{:S(2)}) collective-permute-start(f32[512,256]{0,1:T(8,128)S(1)} %bitcast.26), channel_id=1, source_target_pairs={{8,0},{10,2},{12,4},{14,6},{0,8},{2,10},{4,12},{6,14},{9,1},{11,3}... | collective-permute-start | bytes 1572872 | tf_op jit(solution)/shard_map/ppermute | solution.py:25
  222.9 36.5 %collective-permute-start.4 = (f32[512,256]{0,1:T(8,128)S(1)}, f32[512,256]{0,1:T(8,128)S(1)}, u32[]{:S(2)}, u32[]{:S(2)}) collective-permute-start(f32[512,256]{0,1:T(8,128)S(1)} %bitcast.27), channel_id=1, source_target_pairs={{10,0},{12,2},{14,4},{0,6},{2,8},{4,10},{6,12},{8,14},{11,1},{13,3... | collective-permute-start | bytes 1572872 | tf_op jit(solution)/shard_map/ppermute | solution.py:25
  256.1 16.3 %collective-permute-start.5 = (f32[512,256]{0,1:T(8,128)S(1)}, f32[512,256]{0,1:T(8,128)S(1)}, u32[]{:S(2)}, u32[]{:S(2)}) collective-permute-start(f32[512,256]{0,1:T(8,128)S(1)} %bitcast.28), channel_id=1, source_target_pairs={{12,0},{14,2},{0,4},{2,6},{4,8},{6,10},{8,12},{10,14},{13,1},{15,3... | collective-permute-start | bytes 1572872 | tf_op jit(solution)/shard_map/ppermute | solution.py:25
  256.9 16.3 %collective-permute-start.6 = (f32[512,256]{0,1:T(8,128)S(1)}, f32[512,256]{0,1:T(8,128)S(1)}, u32[]{:S(2)}, u32[]{:S(2)}) collective-permute-start(f32[512,256]{0,1:T(8,128)S(1)} %bitcast.29), channel_id=1, source_target_pairs={{14,0},{0,2},{2,4},{4,6},{6,8},{8,10},{10,12},{12,14},{15,1},{1,3}... | collective-permute-start | bytes 1572872 | tf_op jit(solution)/shard_map/ppermute | solution.py:25
  285.4 50.7 %collective-permute-start.7 = (f32[512,2048]{0,1:T(8,128)}, f32[512,2048]{0,1:T(8,128)}, u32[]{:S(2)}, u32[]{:S(2)}) collective-permute-start(f32[512,2048]{0,1:T(8,128)} %constant_dynamic-slice_fusion.1), channel_id=1, source_target_pairs={{0,16},{18,2},{1,17},{19,3},{4,20},{22,6},{5,21},{23,7},{8,24},{26... | collective-permute-start | bytes 12582920 | tf_op jit(solution)/shard_map/ppermute | solution.py:59
  354.0 27.6 %copy-start.1 = (s32[8,32]{1,0:T(8,128)S(1)}, s32[8,32]{1,0:T(8,128)}, u32[]{:S(2)}) copy-start(s32[8,32]{1,0:T(8,128)} %param.9) | copy-start | bytes 3076
  354.0 34.7 %collective-permute-start.12 = (f32[512,1024]{1,0:T(8,128)}, f32[512,1024]{1,0:T(8,128)}, u32[]{:S(2)}, u32[]{:S(2)}) collective-permute-start(f32[512,1024]{1,0:T(8,128)} %fusion.1), channel_id=1, source_target_pairs={{0,0},{2,17},{16,2},{18,19},{4,4},{6,21},{20,6},{22,23},{8,8},{10,... | collective-permute-start | bytes 6291464 | tf_op jit(solution)/shard_map/ppermute | solution.py:71
  356.8 31.9 %collective-permute-start.13 = (f32[512,1024]{1,0:T(8,128)}, f32[512,1024]{1,0:T(8,128)}, u32[]{:S(2)}, u32[]{:S(2)}) collective-permute-start(f32[512,1024]{1,0:T(8,128)} %fusion.1), channel_id=1, source_target_pairs={{1,0},{3,17},{17,2},{19,19},{5,4},{7,21},{21,6},{23,23},{9,8},{11,... | collective-permute-start | bytes 6291464 | tf_op jit(solution)/shard_map/ppermute | solution.py:71
  376.7 66.0 %collective-permute-start.15 = (f32[512,1024]{1,0:T(8,128)}, f32[512,1024]{1,0:T(8,128)}, u32[]{:S(2)}, u32[]{:S(2)}) collective-permute-start(f32[512,1024]{1,0:T(8,128)} %fusion), channel_id=1, source_target_pairs={{0,1},{2,16},{16,3},{18,18},{4,5},{6,20},{20,7},{22,22},{8,9},{10,... | collective-permute-start | bytes 6291464 | tf_op jit(solution)/shard_map/ppermute | solution.py:71
  380.4 89.6 %collective-permute-start.16 = (f32[512,1024]{1,0:T(8,128)}, f32[512,1024]{1,0:T(8,128)}, u32[]{:S(2)}, u32[]{:S(2)}) collective-permute-start(f32[512,1024]{1,0:T(8,128)} %fusion), channel_id=1, source_target_pairs={{1,1},{3,16},{17,3},{19,18},{5,5},{7,20},{21,7},{23,22},{9,9},{11,... | collective-permute-start | bytes 6291464 | tf_op jit(solution)/shard_map/ppermute | solution.py:71
Sparse Core Ops, SparseCore 0:
  28.9 177.5 all-gather.1
where the time goes:
time: 485 us; the launch traced here: 484 us
  waiting for transfers between devices  375 us (77%)
  matrix products  35.8 us (7%)
  starting transfers between devices  26.4 us (5%)
  local copies, waits for them, and re-layouts  22.2 us (5%)
  between operations  13.6 us (3%)
  other arithmetic  10.7 us (2%)
    all_gather x1, waiting for transfers between devices, shards(): ham_own = lax.all_gather(contrib, ('zl', 'yh'), axis=0, tiled=True)  178 us
    ppermute x4, waiting for transfers between devices, route(): lax.ppermute(value, ('yl', 'core', 'layer'), [p for p in perm if p[0] % 2...  85.5 us
    ppermute x7, waiting for transfers between devices, gather_cols(): lax.ppermute(block, COL, [((i + shift) % n, i) for i in range(n)])  53.4 us
    ppermute x1, waiting for transfers between devices, shards(): dens_nbr = lax.ppermute(dens_own, ('yl', 'core'), [(0, 2), (3, 1)])  49.2 us
    dot_general x2, matrix products, product_dot(): jnp.dot(a, b, precision=lax.Precision.HIGH, preferred_element_type=jnp.fl...  35.8 us
    unnamed x23, local copies, waits for them, and re-layouts  15.3 us
  transfers between devices with their start and end apart: 18, of which 11 were waited for; matrix products, arithmetic and copies ran while one was open for 12% of the time, Pallas kernels for 0%

commit v1 on v0

--- a/solution.py
+++ b/solution.py
@@ -53,7 +53,20 @@
         jnp.concatenate([pieces[0, 0], pieces[0, 1]], axis=0),
         jnp.concatenate([pieces[1, 0], pieces[1, 1]], axis=0),
     )
-    ham_own = lax.all_gather(contrib, ("zl", "yh"), axis=0, tiled=True)
+
+    def advance_fields(local_x, dim_k):
+        u_next = jnp.concatenate(
+            lax.all_to_all(
+                jnp.stack([local_x for _ in range(lax.axis_size(("zl", "yh")))], 0),
+                ("zl", "yh"),
+                0,
+                0,
+            ),
+            dim_k,
+        )
+        return u_next
+
+    ham_own = advance_fields(contrib, 0)
     ham_other = lax.ppermute(ham_own, "core", [(0, 1), (1, 0)])
     dens_own = gather_cols(dens_vals, col, n_col)
     dens_nbr = lax.ppermute(dens_own, ("yl", "core"), [(0, 2), (3, 1)])

time: 485 us -> 475 us (0.979)
  blocking collectives: 0 us -> 183 us
  waiting for transfers between devices: 375 us -> 202 us
  between operations: 13.6 us -> 0.24 us
  matrix products: 35.8 us -> 23.3 us
    all_to_all x0 -> x1, blocking collectives: none -> 183 us  [advance_fields(): lax.all_to_all(jnp.stack([local_x for _ in range(lax.axis_size(('zl', 'yh...]
    all_gather x1 -> x0, waiting for transfers between devices: 178 us -> none  [shards(): ham_own = lax.all_gather(contrib, ('zl', 'yh'), axis=0, tiled=True)]
    dot_general x2, matrix products: 35.8 us -> 23.3 us  [product_dot(): jnp.dot(a, b, precision=lax.Precision.HIGH, preferred_element_type=jnp.fl...]
  transfers between devices with their start and end apart: 18 -> 17, of which waited for: 11 -> 10; matrix products, arithmetic and copies ran while one was open for 12% -> 9% of each run, Pallas kernels for 0% -> 0%
where the time goes in v1:
time: 475 us; the launch traced here: 471 us
  waiting for transfers between devices  202 us (43%)
  blocking collectives  183 us (39%)
  starting transfers between devices  30.2 us (6%)
  local copies, waits for them, and re-layouts  23.5 us (5%)
  matrix products  23.3 us (5%)
  other arithmetic  9.69 us (2%)
    all_to_all x1, blocking collectives, advance_fields(): lax.all_to_all(jnp.stack([local_x for _ in range(lax.axis_size(('zl', 'yh...  183 us
    ppermute x4, waiting for transfers between devices, route(): lax.ppermute(value, ('yl', 'core', 'layer'), [p for p in perm if p[0] % 2...  87.7 us
    ppermute x7, waiting for transfers between devices, gather_cols(): lax.ppermute(block, COL, [((i + shift) % n, i) for i in range(n)])  53.4 us
    ppermute x1, waiting for transfers between devices, shards(): dens_nbr = lax.ppermute(dens_own, ('yl', 'core'), [(0, 2), (3, 1)])  51.7 us
    dot_general x2, matrix products, product_dot(): jnp.dot(a, b, precision=lax.Precision.HIGH, preferred_element_type=jnp.fl...  23.3 us
    unnamed x23, local copies, waits for them, and re-layouts  15.2 us
    ppermute x4, starting transfers between devices, route(): lax.ppermute(value, ('yl', 'core', 'layer'), [p for p in perm if p[0] % 2...  13.6 us
  transfers between devices with their start and end apart: 17, of which 10 were waited for; matrix products, arithmetic and copies ran while one was open for 9% of the time, Pallas kernels for 0%

profile of v1, /device:TPU:104, one launch (start us, length us, event | category | flops | bytes accessed | tf_op | source)
XLA Modules:
  0.0 471.3 jit_solution(1720147452877106249)
XLA Ops:
  1.0 1.6 copy.8
  2.7 0.7 collective-permute-start.10
  3.4 4.3 collective-permute-start.11
  7.7 1.3 collective-permute-start.8
  9.0 1.9 collective-permute-start.9
  11.0 3.4 collective-permute-done.11
  14.4 3.9 collective-permute-done.8
  18.2 1.8 collective-permute-done.9
  20.0 1.1 maximum_select_fusion
  21.5 1.1 stack.2
  22.6 182.6 %all_to_all.5 = f32[8,256,1024]{2,1,0:T(8,128)} all-to-all(f32[8,256,1024]{2,1,0:T(8,128)S(1)} %stack.2), channel_id=1, replica_groups=mesh['zl'=4,'yh'=2,'yl'=2,'x'=4,'core'=2,'layer'=2] {'zl','yh'}, dimensions={0} | all-to-all | bytes 16777216 | tf_op jit(solution)/shard_map/all_to_all | solution.py:59
  205.5 0.9 constant_dynamic-update-slice_fusion.15
  206.5 2.9 collective-permute-start
  209.4 0.8 collective-permute-start.1
  210.2 2.4 collective-permute-start.3
  212.6 9.1 %collective-permute-done = f32[512,256]{0,1:T(8,128)S(1)} collective-permute-done((f32[512,256]{0,1:T(8,128)S(1)}, f32[512,256]{0,1:T(8,128)S(1)}, u32[]{:S(2)}, u32[]{:S(2)}) %collective-permute-start) | collective-permute-done | bytes 524320 | tf_op jit(solution)/shard_map/ppermute | solution.py:25
  221.7 0.9 collective-permute-start.4
  222.6 32.2 %collective-permute-done.1 = f32[512,256]{0,1:T(8,128)S(1)} collective-permute-done((f32[512,256]{0,1:T(8,128)S(1)}, f32[512,256]{0,1:T(8,128)S(1)}, u32[]{:S(2)}, u32[]{:S(2)}) %collective-permute-start.1) | collective-permute-done | bytes 524320 | tf_op jit(solution)/shard_map/ppermute | solution.py:25
  254.8 0.8 constant_dynamic-update-slice_fusion.14
  255.7 0.8 constant_dynamic-update-slice_fusion.13
  256.5 0.8 constant_dynamic-update-slice_fusion.12
  257.4 0.8 constant_dynamic-update-slice_fusion.11
  258.2 0.8 constant_dynamic-update-slice_fusion.10
  259.0 12.1 %collective-permute-done.5 = f32[512,256]{0,1:T(8,128)S(1)} collective-permute-done((f32[512,256]{0,1:T(8,128)S(1)}, f32[512,256]{0,1:T(8,128)S(1)}, u32[]{:S(2)}, u32[]{:S(2)}) %collective-permute-start.5) | collective-permute-done | bytes 524320 | tf_op jit(solution)/shard_map/ppermute | solution.py:25
  271.1 0.8 constant_dynamic-update-slice_fusion.9
  271.9 0.8 constant_dynamic-update-slice_fusion.8
  272.8 0.8 constant_dynamic-update-slice_fusion.7
  273.6 0.8 constant_dynamic-update-slice_fusion.6
  274.4 0.8 constant_dynamic-update-slice_fusion.5
  275.3 0.9 constant_dynamic-update-slice_fusion.4
  276.1 0.8 constant_dynamic-update-slice_fusion.3
  276.9 0.8 constant_dynamic-update-slice_fusion.2
  277.8 0.8 constant_dynamic-update-slice_fusion.1
  278.6 0.9 constant_dynamic-update-slice_fusion
  279.5 4.6 constant_dynamic-slice_fusion.1
  284.1 1.3 collective-permute-start.7
  285.4 51.7 %collective-permute-done.7 = f32[512,2048]{0,1:T(8,128)} collective-permute-done((f32[512,2048]{0,1:T(8,128)}, f32[512,2048]{0,1:T(8,128)}, u32[]{:S(2)}, u32[]{:S(2)}) %collective-permute-start.7) | collective-permute-done | bytes 4194336 | tf_op jit(solution)/shard_map/ppermute | solution.py:72
  337.1 11.6 %fusion.1 = f32[512,1024]{1,0:T(8,128)} fusion(f32[2048,1024]{1,0:T(8,128)} %bitcast.6, f32[512,2048]{0,1:T(8,128)} %constant_dynamic-slice_fusion.1, f32[512,2048]{0,1:T(8,128)} %collective-permute-done.7, pred[]{:T(512)S(6)} %eq.6), kind=kOutput, calls=%fused_computation.3 | convolution fusion | flops 6443499520 | bytes 18874368 | tf_op jit(solution)/shard_map/dot_general | solution.py:19
  348.7 2.8 collective-permute-start.12
  351.5 2.0 collective-permute-start.13
  353.5 11.7 %fusion = f32[512,1024]{1,0:T(8,128)} fusion(f32[2048,1024]{1,0:T(8,128)} %collective-permute-done.14, f32[512,2048]{0,1:T(8,128)} %constant_dynamic-slice_fusion.1, f32[512,2048]{0,1:T(8,128)} %collective-permute-done.7, pred[]{:T(512)S(6)} %eq.6), kind=kOutput, calls=%fused_computation.2 | convolution fusion | flops 6443499520 | bytes 18874368 | tf_op jit(solution)/shard_map/dot_general | solution.py:19
  365.2 7.5 %collective-permute-start.15 = (f32[512,1024]{1,0:T(8,128)}, f32[512,1024]{1,0:T(8,128)}, u32[]{:S(2)}, u32[]{:S(2)}) collective-permute-start(f32[512,1024]{1,0:T(8,128)} %fusion), channel_id=1, source_target_pairs={{0,1},{2,16},{16,3},{18,18},{4,5},{6,20},{20,7},{22,22},{8,9},{10,... | collective-permute-start | bytes 6291464 | tf_op jit(solution)/shard_map/ppermute | solution.py:84
  372.7 1.3 collective-permute-start.16
  375.0 1.8 copy.13
  376.8 10.4 %collective-permute-done.12 = f32[512,1024]{1,0:T(8,128)} collective-permute-done((f32[512,1024]{1,0:T(8,128)}, f32[512,1024]{1,0:T(8,128)}, u32[]{:S(2)}, u32[]{:S(2)}) %collective-permute-start.12) | collective-permute-done | bytes 2097184 | tf_op jit(solution)/shard_map/ppermute | solution.py:84
  387.2 54.2 %collective-permute-done.15 = f32[512,1024]{1,0:T(8,128)} collective-permute-done((f32[512,1024]{1,0:T(8,128)}, f32[512,1024]{1,0:T(8,128)}, u32[]{:S(2)}, u32[]{:S(2)}) %collective-permute-start.15) | collective-permute-done | bytes 2097184 | tf_op jit(solution)/shard_map/ppermute | solution.py:84
  441.3 23.1 %collective-permute-done.16 = f32[512,1024]{1,0:T(8,128)} collective-permute-done((f32[512,1024]{1,0:T(8,128)}, f32[512,1024]{1,0:T(8,128)}, u32[]{:S(2)}, u32[]{:S(2)}) %collective-permute-start.16) | collective-permute-done | bytes 2097184 | tf_op jit(solution)/shard_map/ppermute | solution.py:84
  464.4 6.8 %add_multiply_fusion = f32[512,1024]{1,0:T(8,128)} fusion(f32[512,1024]{1,0:T(8,128)} %copy.13, f32[512,1024]{1,0:T(8,128)} %collective-permute-done.15, f32[512,1024]{1,0:T(8,128)} %collective-permute-done.16, f32[512,1024]{1,0:T(8,128)} %collective-permute-done.12, f32[512,1024]{1,0:T(8,128)} %collective-permute-done.13), kind=kLoop, calls=%fused_computation | loop fusion | flops 2097152 | bytes 12582912 | tf_op jit(solution)/shard_map/mul | solution.py:90
  (34 shorter events, 2.8 us)
Async XLA Ops:
  2.7 8.3 %collective-permute-start.10 = (f32[128,1024]{0,1:T(8,128)S(1)}, f32[128,1024]{0,1:T(8,128)S(1)}, u32[]{:S(2)}, u32[]{:S(2)}) collective-permute-start(f32[128,1024]{0,1:T(8,128)S(1)} %get-tuple-element.5), channel_id=1, source_target_pairs={{0,2},{2,18},{1,3},{3,19},{4,6},{6,22},{5,7},{7,23},{8,10},{10,26}... | collective-permute-start | bytes 1572872 | tf_op jit(solution)/shard_map/ppermute | solution.py:48
  3.4 11.0 %collective-permute-start.11 = (f32[128,1024]{0,1:T(8,128)S(1)}, f32[128,1024]{0,1:T(8,128)S(1)}, u32[]{:S(2)}, u32[]{:S(2)}) collective-permute-start(f32[128,1024]{0,1:T(8,128)S(1)} %get-tuple-element.5), channel_id=1, source_target_pairs={{16,2},{18,18},{17,3},{19,19},{20,6},{22,22},{21,7},{23,23},{24,10... | collective-permute-start | bytes 1572872 | tf_op jit(solution)/shard_map/ppermute | solution.py:48
  7.7 10.5 %collective-permute-start.8 = (f32[128,1024]{0,1:T(8,128)S(1)}, f32[128,1024]{0,1:T(8,128)S(1)}, u32[]{:S(2)}, u32[]{:S(2)}) collective-permute-start(f32[128,1024]{0,1:T(8,128)S(1)} %get-tuple-element.6), channel_id=1, source_target_pairs={{0,0},{2,16},{1,1},{3,17},{4,4},{6,20},{5,5},{7,21},{8,8},{10,24},... | collective-permute-start | bytes 1572872 | tf_op jit(solution)/shard_map/ppermute | solution.py:48
  9.0 11.0 %collective-permute-start.9 = (f32[128,1024]{0,1:T(8,128)S(1)}, f32[128,1024]{0,1:T(8,128)}, u32[]{:S(2)}, u32[]{:S(2)}) collective-permute-start(f32[128,1024]{0,1:T(8,128)S(1)} %get-tuple-element.6), channel_id=1, source_target_pairs={{16,0},{18,16},{17,1},{19,17},{20,4},{22,20},{21,5},{23,21},{24,8}... | collective-permute-start | bytes 1572872 | tf_op jit(solution)/shard_map/ppermute | solution.py:48
  22.5 182.6 %copy-start = (f32[1,512,256]{2,1,0:T(8,128)S(1)}, f32[1,512,256]{2,1,0:T(8,128)}, u32[]{:S(2)}) copy-start(f32[1,512,256]{2,1,0:T(8,128)} %param.5) | copy-start | bytes 1572868
  22.6 182.8 %copy-start.2 = (s32[1,8,4]{1,2,0:T(4,128)S(1)}, s32[1,8,4]{1,2,0:T(4,128)}, u32[]{:S(2)}) copy-start(s32[1,8,4]{1,2,0:T(4,128)} %param.6) | copy-start | bytes 388
  205.2 148.4 %collective-permute-start.14 = (f32[2048,1024]{1,0:T(8,128)}, f32[2048,1024]{1,0:T(8,128)}, u32[]{:S(2)}, u32[]{:S(2)}) collective-permute-start(f32[2048,1024]{1,0:T(8,128)} %bitcast.6), channel_id=1, source_target_pairs={{0,2},{2,0},{1,3},{3,1},{4,6},{6,4},{5,7},{7,5},{8,10},{10,8},{9,1... | collective-permute-start | bytes 25165832 | tf_op jit(solution)/shard_map/ppermute | solution.py:70
  206.5 15.2 %collective-permute-start = (f32[512,256]{0,1:T(8,128)S(1)}, f32[512,256]{0,1:T(8,128)S(1)}, u32[]{:S(2)}, u32[]{:S(2)}) collective-permute-start(f32[512,256]{0,1:T(8,128)S(1)} %bitcast.24), channel_id=1, source_target_pairs={{2,0},{4,2},{6,4},{8,6},{10,8},{12,10},{14,12},{0,14},{3,1},{5,3},... | collective-permute-start | bytes 1572872 | tf_op jit(solution)/shard_map/ppermute | solution.py:25
  209.4 45.5 %collective-permute-start.1 = (f32[512,256]{0,1:T(8,128)S(1)}, f32[512,256]{0,1:T(8,128)S(1)}, u32[]{:S(2)}, u32[]{:S(2)}) collective-permute-start(f32[512,256]{0,1:T(8,128)S(1)} %bitcast.25), channel_id=1, source_target_pairs={{4,0},{6,2},{8,4},{10,6},{12,8},{14,10},{0,12},{2,14},{5,1},{7,3},... | collective-permute-start | bytes 1572872 | tf_op jit(solution)/shard_map/ppermute | solution.py:25
  210.2 45.5 %collective-permute-start.2 = (f32[512,256]{0,1:T(8,128)S(1)}, f32[512,256]{0,1:T(8,128)S(1)}, u32[]{:S(2)}, u32[]{:S(2)}) collective-permute-start(f32[512,256]{0,1:T(8,128)S(1)} %bitcast.26), channel_id=1, source_target_pairs={{6,0},{8,2},{10,4},{12,6},{14,8},{0,10},{2,12},{4,14},{7,1},{9,3},... | collective-permute-start | bytes 1572872 | tf_op jit(solution)/shard_map/ppermute | solution.py:25
  210.2 47.2 %collective-permute-start.3 = (f32[512,256]{0,1:T(8,128)S(1)}, f32[512,256]{0,1:T(8,128)S(1)}, u32[]{:S(2)}, u32[]{:S(2)}) collective-permute-start(f32[512,256]{0,1:T(8,128)S(1)} %bitcast.27), channel_id=1, source_target_pairs={{8,0},{10,2},{12,4},{14,6},{0,8},{2,10},{4,12},{6,14},{9,1},{11,3}... | collective-permute-start | bytes 1572872 | tf_op jit(solution)/shard_map/ppermute | solution.py:25
  221.7 36.5 %collective-permute-start.4 = (f32[512,256]{0,1:T(8,128)S(1)}, f32[512,256]{0,1:T(8,128)S(1)}, u32[]{:S(2)}, u32[]{:S(2)}) collective-permute-start(f32[512,256]{0,1:T(8,128)S(1)} %bitcast.28), channel_id=1, source_target_pairs={{10,0},{12,2},{14,4},{0,6},{2,8},{4,10},{6,12},{8,14},{11,1},{13,3... | collective-permute-start | bytes 1572872 | tf_op jit(solution)/shard_map/ppermute | solution.py:25
  254.8 16.3 %collective-permute-start.5 = (f32[512,256]{0,1:T(8,128)S(1)}, f32[512,256]{0,1:T(8,128)S(1)}, u32[]{:S(2)}, u32[]{:S(2)}) collective-permute-start(f32[512,256]{0,1:T(8,128)S(1)} %bitcast.29), channel_id=1, source_target_pairs={{12,0},{14,2},{0,4},{2,6},{4,8},{6,10},{8,12},{10,14},{13,1},{15,3... | collective-permute-start | bytes 1572872 | tf_op jit(solution)/shard_map/ppermute | solution.py:25
  255.7 16.3 %collective-permute-start.6 = (f32[512,256]{0,1:T(8,128)S(1)}, f32[512,256]{0,1:T(8,128)S(1)}, u32[]{:S(2)}, u32[]{:S(2)}) collective-permute-start(f32[512,256]{0,1:T(8,128)S(1)} %bitcast.30), channel_id=1, source_target_pairs={{14,0},{0,2},{2,4},{4,6},{6,8},{8,10},{10,12},{12,14},{15,1},{1,3}... | collective-permute-start | bytes 1572872 | tf_op jit(solution)/shard_map/ppermute | solution.py:25
  284.1 53.0 %collective-permute-start.7 = (f32[512,2048]{0,1:T(8,128)}, f32[512,2048]{0,1:T(8,128)}, u32[]{:S(2)}, u32[]{:S(2)}) collective-permute-start(f32[512,2048]{0,1:T(8,128)} %constant_dynamic-slice_fusion.1), channel_id=1, source_target_pairs={{0,16},{18,2},{1,17},{19,3},{4,20},{22,6},{5,21},{23,7},{8,24},{26... | collective-permute-start | bytes 12582920 | tf_op jit(solution)/shard_map/ppermute | solution.py:72
  348.7 25.3 %copy-start.1 = (s32[8,32]{1,0:T(8,128)S(1)}, s32[8,32]{1,0:T(8,128)}, u32[]{:S(2)}) copy-start(s32[8,32]{1,0:T(8,128)} %param.9) | copy-start | bytes 3076
  348.7 38.4 %collective-permute-start.12 = (f32[512,1024]{1,0:T(8,128)}, f32[512,1024]{1,0:T(8,128)}, u32[]{:S(2)}, u32[]{:S(2)}) collective-permute-start(f32[512,1024]{1,0:T(8,128)} %fusion.1), channel_id=1, source_target_pairs={{0,0},{2,17},{16,2},{18,19},{4,4},{6,21},{20,6},{22,23},{8,8},{10,... | collective-permute-start | bytes 6291464 | tf_op jit(solution)/shard_map/ppermute | solution.py:84
  351.5 35.7 %collective-permute-start.13 = (f32[512,1024]{1,0:T(8,128)}, f32[512,1024]{1,0:T(8,128)}, u32[]{:S(2)}, u32[]{:S(2)}) collective-permute-start(f32[512,1024]{1,0:T(8,128)} %fusion.1), channel_id=1, source_target_pairs={{1,0},{3,17},{17,2},{19,19},{5,4},{7,21},{21,6},{23,23},{9,8},{11,... | collective-permute-start | bytes 6291464 | tf_op jit(solution)/shard_map/ppermute | solution.py:84
  365.2 76.2 %collective-permute-start.15 = (f32[512,1024]{1,0:T(8,128)}, f32[512,1024]{1,0:T(8,128)}, u32[]{:S(2)}, u32[]{:S(2)}) collective-permute-start(f32[512,1024]{1,0:T(8,128)} %fusion), channel_id=1, source_target_pairs={{0,1},{2,16},{16,3},{18,18},{4,5},{6,20},{20,7},{22,22},{8,9},{10,... | collective-permute-start | bytes 6291464 | tf_op jit(solution)/shard_map/ppermute | solution.py:84
  372.7 91.8 %collective-permute-start.16 = (f32[512,1024]{1,0:T(8,128)}, f32[512,1024]{1,0:T(8,128)}, u32[]{:S(2)}, u32[]{:S(2)}) collective-permute-start(f32[512,1024]{1,0:T(8,128)} %fusion), channel_id=1, source_target_pairs={{1,1},{3,16},{17,3},{19,18},{5,5},{7,20},{21,7},{23,22},{9,9},{11,... | collective-permute-start | bytes 6291464 | tf_op jit(solution)/shard_map/ppermute | solution.py:84
